TPU v7x, 256 devices: a whole 4x4x8 slice. The times are simulated.
256 devices in a mesh: batch: 8 (over z), replica: 32 (over y, x, core).
Axes of the slice: x: 4, y: 4, z: 8, core: 2. Of those that a mesh axis runs over, the one named last changes fastest.
Arguments:
- patches: bfloat16 [32, 64, 64, 1024], P('replica', 'batch'), may hold values from -6 to 6
- visible_order: int32 [32, 64, 64], P('replica', 'batch'), may hold values from 0 to 63, each once within a row
- visible_counts: int32 [32, 64], P('replica'), may hold values from 1 to 32, as said below
- dest_rows: int32 [32, 64], P('replica'), may hold values from 0 to 1023, as said below
- qkv_weight: bfloat16 [1024, 3072], P('replica')
- out_weight: bfloat16 [1024, 1024], P('replica'), may hold values from -0.1875 to 0.1875
- norm_gain: bfloat16 [1024], P('replica'), may hold values from 0.5 to 1.5
- upstream: bfloat16 [32, 1024, 1024], P('replica', 'batch'), may hold values from -6 to 6
Outputs:
- layer_out: bfloat16 [32, 1024, 1024], P('replica', 'batch')
- d_packed: bfloat16 [32, 1024, 1024], P('replica', 'batch')
- grad_qkv: float32 [1024, 3072], P('replica')
- grad_out: float32 [1024, 1024], P('replica')
- grad_gain: float32 [1024], P('replica')
Inputs may be any that keep to these rules, and one draw needn't show every extreme that they name: `visible_counts`: in every replica index, each batch index b packs exactly 128 rows: the volumes with dest_rows // 128 == b, one from every device of the batch axis, in order of that device's batch index, without gaps; one of them has 32 visible patches. `dest_rows`: the 8 volumes of one device go to 8 different batch indices; a volume's rows never cross a multiple of 128.
All inputs are finite; a program needn't handle non-finite values.
Results may differ from a plain program's by a relative error of at most 0.033.
Values may be sent and summed in bfloat16 or wider, within the bound.
No kernel may reach another device: no remote copies, remote signals or barrier semaphores. Data moves between devices by JAX's collectives and lax.ppermute only.
A program may use at most 128 MiB of HBM per device.

v0:
```python
import jax
import jax.numpy as jnp
from jax import lax
from jax.sharding import PartitionSpec as P

HEADS = 16
MAXVIS = 32
MEANVIS = 16
EPS = 1e-06
NEG = -1e30


def layer_core(tokens, upward, allowed, wqkv, wout, gain):
    groups, length, width = tokens.shape
    rows = groups * length
    head_dim = width // HEADS
    scale = head_dim ** (-0.5)
    x32 = tokens.astype(jnp.float32).reshape(rows, width)
    row_average = jnp.mean(x32, axis=1, keepdims=True)
    centered_rows = x32 - row_average
    inverse_deviation = lax.rsqrt(
        jnp.mean(centered_rows * centered_rows, axis=1, keepdims=True) + EPS
    )
    standardized_rows = centered_rows * inverse_deviation
    gain_float32 = gain.astype(jnp.float32)
    layernorm_output = (standardized_rows * gain_float32).astype(jnp.bfloat16)
    qkv = jnp.dot(layernorm_output, wqkv, preferred_element_type=jnp.float32).astype(jnp.bfloat16)
    query = qkv[:, :width].reshape(groups, length, HEADS, head_dim)
    keys = qkv[:, width : 2 * width].reshape(groups, length, HEADS, head_dim)
    values = qkv[:, 2 * width :].reshape(groups, length, HEADS, head_dim)
    scores = jnp.einsum("gqhd,gkhd->ghqk", query, keys, preferred_element_type=jnp.float32) * scale
    scores = jnp.where(allowed[:, None], scores, NEG)
    top = jnp.max(scores, axis=-1, keepdims=True)
    expd = jnp.exp(scores - top)
    probs = expd / jnp.sum(expd, axis=-1, keepdims=True)
    weights = probs.astype(jnp.bfloat16)
    context = (
        jnp.einsum("ghqk,gkhd->gqhd", weights, values, preferred_element_type=jnp.float32)
        .astype(jnp.bfloat16)
        .reshape(rows, width)
    )
    result = (x32 + jnp.dot(context, wout, preferred_element_type=jnp.float32)).astype(jnp.bfloat16)
    up_rows = upward.reshape(rows, width)
    d_context = lax.dot_general(
        up_rows, wout, (((1,), (1,)), ((), ())), preferred_element_type=jnp.float32
    ).astype(jnp.bfloat16)
    d_context = d_context.reshape(groups, length, HEADS, head_dim)
    d_values = jnp.einsum(
        "ghqk,gqhd->gkhd", weights, d_context, preferred_element_type=jnp.float32
    ).astype(jnp.bfloat16)
    d_weights = jnp.einsum("gqhd,gkhd->ghqk", d_context, values, preferred_element_type=jnp.float32)
    d_scores = (
        probs * (d_weights - jnp.sum(d_weights * probs, axis=-1, keepdims=True)) * scale
    ).astype(jnp.bfloat16)
    d_query = jnp.einsum(
        "ghqk,gkhd->gqhd", d_scores, keys, preferred_element_type=jnp.float32
    ).astype(jnp.bfloat16)
    d_keys = jnp.einsum(
        "ghqk,gqhd->gkhd", d_scores, query, preferred_element_type=jnp.float32
    ).astype(jnp.bfloat16)
    d_qkv = jnp.concatenate(
        [d_query.reshape(rows, width), d_keys.reshape(rows, width), d_values.reshape(rows, width)],
        axis=1,
    )
    layernorm_gradient = lax.dot_general(
        d_qkv, wqkv, (((1,), (1,)), ((), ())), preferred_element_type=jnp.float32
    )
    gain_products = jnp.sum(layernorm_gradient * standardized_rows, axis=0)
    normalized_gradient = layernorm_gradient * gain_float32
    input_gradient = inverse_deviation * (
        normalized_gradient
        - jnp.mean(normalized_gradient, axis=1, keepdims=True)
        - standardized_rows
        * jnp.mean(normalized_gradient * standardized_rows, axis=1, keepdims=True)
    )
    d_tokens = (up_rows.astype(jnp.float32) + input_gradient).astype(jnp.bfloat16)
    return (
        result.reshape(tokens.shape),
        d_tokens.reshape(tokens.shape),
        layernorm_output,
        context,
        d_qkv,
        up_rows,
        gain_products,
    )


def left_product(left, right):
    return lax.dot_general(
        left, right, (((0,), (0,)), ((), ())), preferred_element_type=jnp.float32
    )


def on_device(
    patches, visible_order, visible_counts, dest_rows, qkv_weight, out_weight, norm_gain, upstream
):
    qkv_cols = qkv_weight.shape[1]
    out_cols = out_weight.shape[1]
    gain_block = jnp.broadcast_to(norm_gain[:, None], (norm_gain.shape[0], 128))
    gathered = lax.all_gather(
        jnp.concatenate([qkv_weight, out_weight, gain_block], axis=1), "replica", axis=0, tiled=True
    )
    wqkv = gathered[:, :qkv_cols]
    wout = gathered[:, qkv_cols : qkv_cols + out_cols]
    gain = gathered[:, qkv_cols + out_cols]
    batches = lax.axis_size("batch")
    me_index = lax.axis_index("batch")
    cap = MEANVIS * batches
    width = wout.shape[1]
    slot = jnp.arange(MAXVIS, dtype=jnp.int32)
    sources = jnp.arange(batches, dtype=jnp.int32)
    counts_all = visible_counts[0].reshape(batches, batches)
    rows_all = dest_rows[0].reshape(batches, batches)
    mine = rows_all // cap == me_index
    src_count = jnp.sum(jnp.where(mine, counts_all, 0), axis=1)
    src_start = jnp.sum(jnp.where(mine, rows_all % cap, 0), axis=1)
    position = jnp.arange(cap, dtype=jnp.int32)
    hit = (position[:, None] >= src_start[None, :]) & (
        position[:, None] < (src_start + src_count)[None, :]
    )
    segment = jnp.sum(jnp.where(hit, sources[None, :], 0), axis=1)
    inside = jnp.sum(jnp.where(hit, position[:, None] - src_start[None, :], 0), axis=1)
    flat_rows = segment * MAXVIS + inside
    my_targets = jnp.take(rows_all, me_index, axis=0) // cap
    to_target = jnp.sum(
        jnp.where(my_targets[None, :] == sources[:, None], sources[None, :], 0), axis=1
    )
    my_counts = jnp.take(counts_all, me_index, axis=0)
    local_rows = jnp.take_along_axis(patches[0], visible_order[0, :, :MAXVIS, None], axis=1)
    live = slot[None, :] < src_count[:, None]
    pick = jnp.clip(src_start[:, None] + slot[None, :], 0, cap - 1)
    fetched = jnp.take(upstream[0], pick.reshape(-1), axis=0).reshape(batches, MAXVIS, width)
    backward_rows = jnp.where(live[..., None], fetched, jnp.zeros_like(fetched))
    returned = lax.all_to_all(backward_rows, "batch", split_axis=0, concat_axis=0, tiled=True)
    upward = jnp.take(returned, my_targets, axis=0)
    valid = slot[None, :] < my_counts[:, None]
    allowed = jnp.broadcast_to(valid[:, None, :], (batches, MAXVIS, MAXVIS))
    result, d_tokens, layernorm_output, context, d_qkv, up_rows, gain_products = layer_core(
        local_rows, upward, allowed, wqkv, wout, gain
    )
    came = lax.all_to_all(
        jnp.take(jnp.concatenate([result, d_tokens], axis=-1), to_target, axis=0),
        "batch",
        split_axis=0,
        concat_axis=0,
        tiled=True,
    )
    came_out = came[..., :width]
    came_grad = came[..., width:]
    layer_out = jnp.take(came_out.reshape(batches * MAXVIS, width), flat_rows, axis=0)
    d_packed = jnp.take(came_grad.reshape(batches * MAXVIS, width), flat_rows, axis=0)
    partial = jnp.concatenate(
        [
            left_product(layernorm_output, d_qkv).astype(jnp.bfloat16),
            left_product(context, up_rows).astype(jnp.bfloat16),
            jnp.broadcast_to(gain_products.astype(jnp.bfloat16)[:, None], (width, 128)),
        ],
        axis=1,
    )
    summed = lax.psum_scatter(partial, "replica", scatter_dimension=0, tiled=True)
    summed = lax.psum(summed, "batch").astype(jnp.float32)
    grad_q = summed[:, :qkv_cols]
    grad_o = summed[:, qkv_cols : qkv_cols + out_cols]
    grad_g = summed[:, qkv_cols + out_cols]
    return (layer_out[None], d_packed[None], grad_q, grad_o, grad_g)


def solution(mesh):
    placed = (
        P("replica", "batch", None, None),
        P("replica", "batch", None),
        P("replica", None),
        P("replica", None),
        P("replica", None),
        P("replica", None),
        P("replica"),
        P("replica", "batch", None),
    )
    return jax.shard_map(
        on_device,
        mesh=mesh,
        in_specs=placed,
        out_specs=(
            P("replica", "batch", None),
            P("replica", "batch", None),
            P("replica", None),
            P("replica", None),
            P("replica"),
        ),
        check_vma=False,
    )
```

profile of v0, /device:TPU:2, one launch (start us, length us, event | category | flops | bytes accessed | tf_op | source)
XLA Modules:
  0.0 334.6 jit_solution(9900112664250814567)
XLA Ops:
  8.1 1.7 pad_maximum_fusion.2
  10.3 1.3 reduce.13
  11.7 1.3 reduce.12
  13.5 1.2 gather_fusion
  14.7 1.0 select_select_fusion
  15.7 8.5 %all-to-all-start = ((bf16[8,32,1024]{2,1,0:T(8,128)(2,1)}), bf16[8,32,1024]{2,1,0:T(8,128)(2,1)S(1)}, u32[]{:S(2)}, u32[]{:S(2)}) async-start(bf16[8,32,1024]{2,1,0:T(8,128)(2,1)} %select_select_fusion), calls=%async_computation | async-start | bytes 1048576 | tf_op jit(solution)/shard_map/all_to_all | solution.py:134
  24.3 2.8 gather_fusion.3
  28.2 13.4 %all-to-all-done = bf16[8,32,1024]{2,1,0:T(8,128)(2,1)S(1)} async-done(((bf16[8,32,1024]{2,1,0:T(8,128)(2,1)}), bf16[8,32,1024]{2,1,0:T(8,128)(2,1)S(1)}, u32[]{:S(2)}, u32[]{:S(2)}) %all-to-all-start) | async-done | bytes 524320 | tf_op jit(solution)/shard_map/all_to_all | solution.py:134
  42.2 0.9 broadcast_select_fusion.1
  43.3 29.1 %all-gather.2.cloned.1.call-done = bf16[1024,4224]{1,0:T(8,128)(2,1)} async-done(((bf16[32,4224]{1,0:T(8,128)(2,1)}), bf16[1024,4224]{1,0:T(8,128)(2,1)}) %all-gather.2.cloned.1.call-update) | async-done | bytes 8650768 | tf_op jit(solution)/shard_map/all_gather | solution.py:100
  72.4 3.2 fusion.43
  75.6 1.8 reshape.307
  77.3 1.1 convert_reduce_fusion.1
  78.4 4.7 %fusion.6 = bf16[256,3072]{1,0:T(8,128)(2,1)S(1)} fusion(bf16[1024,4224]{1,0:T(8,128)(2,1)} %all-gather.2.cloned.1.call-done, f32[1024]{0:T(1024)S(1)} %convert_reduce_fusion.1, f32[256]{0:T(256)S(1)} %rsqrt.12, f32[256]{0:T(256)S(1)} %div.51, bf16[256,1024]{1,0:T(8,128)(2,1)S(1)} %gather_fusion.3, pred[256]{0:T(512)(128)(4,1)S(1)} %compare_and_fusion.4), kind=kOutput, calls=%fused_computation.14 | convolution fusion | flops 1612972032 | bytes 8395008 | tf_op jit(solution)/shard_map/dot_general | solution.py:27
  83.2 1.2 fusion.109
  84.4 2.5 reshape.302
  86.9 2.5 reshape.304
  89.4 2.5 reshape.303
  91.9 3.2 fusion.66
  95.1 4.1 %fusion.111 = (f32[8,16,32]{2,1,0:T(8,128)S(1)}, f32[8,16,32,32]{2,3,1,0:T(8,128)}) fusion(pred[8,32]{1,0:T(8,128)(4,1)S(1)} %iota_compare_fusion.3, bf16[8,32,16,64]{3,2,1,0:T(8,128)(2,1)} %reshape.304, bf16[8,32,16,64]{3,2,1,0:T(8,128)(2,1)} %reshape.303), kind=kOutput, calls=%fused_computation.155 | convolution fusion | flops 17301536 | bytes 1589504 | tf_op jit(solution)/shard_map/sub | solution.py:34
  99.2 5.8 %fusion.34 = bf16[8,32,16,64]{3,1,2,0:T(8,128)(2,1)} fusion(f32[8,16,32,32]{2,3,1,0:T(8,128)} %fusion.66, bf16[8,32,16,64]{3,2,1,0:T(8,128)(2,1)} %reshape.304, f32[8,16,32,32]{2,3,1,0:T(8,128)} %get-tuple-element.37, f32[8,16,32]{2,1,0:T(8,128)S(1)} %get-tuple-element.36), kind=kOutput, calls=%fused_computation.35 | convolution fusion | flops 17960992 | bytes 2113536 | tf_op jit(solution)/shard_map/ghqk,gkhd->gqhd/dot_general | solution.py:55
  104.9 5.6 %fusion.31 = bf16[8,32,16,64]{3,1,2,0:T(8,128)(2,1)} fusion(f32[8,16,32,32]{2,3,1,0:T(8,128)} %fusion.66, bf16[8,32,16,64]{3,2,1,0:T(8,128)(2,1)} %reshape.303, f32[8,16,32,32]{2,3,1,0:T(8,128)} %get-tuple-element.37, f32[8,16,32]{2,1,0:T(8,128)S(1)} %get-tuple-element.36), kind=kOutput, calls=%fused_computation.34 | convolution fusion | flops 17960992 | bytes 2113536 | tf_op jit(solution)/shard_map/ghqk,gqhd->gkhd/dot_general | solution.py:58
  110.6 3.2 fusion.30
  113.8 1.6 fusion.29
  115.8 1.5 reshape.308
  117.3 1.9 constant_dynamic-update-slice_fusion.2
  119.2 1.6 copy.50
  120.9 1.5 reshape.309
  122.4 1.6 copy.52
  124.1 1.5 reshape.310
  125.6 1.6 copy.43
  127.2 1.5 reshape.305
  128.7 1.9 constant_dynamic-update-slice_fusion.1
  130.7 1.9 constant_dynamic-update-slice_fusion
  132.6 3.5 %convolution_convert_fusion = bf16[1024,3072]{1,0:T(8,128)(2,1)S(1)} fusion(bf16[256,3072]{1,0:T(8,128)(2,1)} %constant_dynamic-update-slice_fusion, f32[1024]{0:T(1024)S(1)} %convert_reduce_fusion.1, f32[256]{0:T(256)S(1)} %rsqrt.12, f32[256]{0:T(256)S(1)} %div.51, bf16[256,1024]{1,0:T(8,128)(2,1)S(1)} %gather_fusion.3, pred[256]{0:T(512)(128)(4,1)S(1)} %compare_and_fusion.4), kind=kOutput, calls=%fused_computation.9 | convolution fusion | flops 1615331328 | bytes 8395008 | tf_op jit(solution)/shard_map/dot_general | solution.py:89
  136.1 1.0 convolution_convert_fusion.1
  137.5 5.8 %fusion.57 = (bf16[1024]{0:T(1024)(128)(2,1)S(1)}, f32[256]{0:T(256)S(1)}, f32[256]{0:T(256)S(1)}, f32[256,1024]{1,0:T(8,128)}) fusion(f32[256]{0:T(256)S(1)} %rsqrt.12, f32[256]{0:T(256)S(1)} %div.51, bf16[256,1024]{1,0:T(8,128)(2,1)S(1)} %gather_fusion.3, pred[256]{0:T(512)(128)(4,1)S(1)} %compare_and_fusion.4, f32[1024]{0:T(1024)S(1)} %convert_reduce_fusion.1, ...), kind=kOutput, calls=%fused_computation.53 | convolution fusion | flops 1613232640 | bytes 9447680 | tf_op jit(solution)/shard_map/dot_general | solution.py:65
  143.5 3.7 %pad_maximum_fusion = bf16[1024,4224]{1,0:T(8,128)(2,1)} fusion(bf16[1024,128]{1,0:T(8,128)(2,1)S(1)} %broadcast_in_dim.181, bf16[1024,1024]{1,0:T(8,128)(2,1)S(1)} %convolution_convert_fusion.1, bf16[1024,3072]{1,0:T(8,128)(2,1)S(1)} %convolution_convert_fusion), kind=kLoop, calls=%fused_computation.8 | loop fusion | flops 25952256 | bytes 17301504 | tf_op jit(solution)/shard_map/concatenate | solution.py:152
  147.5 1.7 fusion.56
  149.2 2.3 fusion.40
  152.3 1.2 broadcast_select_fusion
  153.4 7.0 %all-to-all-start.1 = ((bf16[8,32,2048]{2,1,0:T(8,128)(2,1)}), bf16[8,32,2048]{2,1,0:T(8,128)(2,1)S(1)}, u32[]{:S(2)}, u32[]{:S(2)}) async-start(bf16[8,32,2048]{2,1,0:T(8,128)(2,1)} %broadcast_select_fusion), calls=%async_computation.1 | async-start | bytes 2097152 | tf_op jit(solution)/shard_map/all_to_all | solution.py:141
  160.5 87.6 %reduce-scatter.2.cloned.1.call-done = bf16[32,4224]{1,0:T(8,128)(2,1)} async-done(((bf16[1024,4224]{1,0:T(8,128)(2,1)}), bf16[32,4224]{1,0:T(8,128)(2,1)}) %reduce-scatter.2.cloned.1.call-update) | async-done | bytes 270352 | tf_op jit(solution)/shard_map/reduce_scatter | solution.py:160
  249.9 0.9 select_bitcast_fusion
  250.8 72.4 %all-reduce.2.cloned.1.call-done = bf16[32,4224]{1,0:T(8,128)(2,1)} async-done(((bf16[32,4224]{1,0:T(8,128)(2,1)}), bf16[32,4224]{1,0:T(8,128)(2,1)}) %all-reduce.2.cloned.1.call-update) | async-done | bytes 270352 | tf_op jit(solution)/shard_map/psum | solution.py:161
  323.3 1.0 convert_element_type.105
  324.9 1.7 slice.75
  326.6 1.5 slice.76
  (72 shorter events, 8.4 us)
Async XLA Ops:
  7.2 17.1 %copy-start = (bf16[1,8,64,1024]{3,2,1,0:T(8,128)(2,1)S(1)}, bf16[1,8,64,1024]{3,2,1,0:T(8,128)(2,1)}, u32[]{:S(2)}) copy-start(bf16[1,8,64,1024]{3,2,1,0:T(8,128)(2,1)} %param.12) | copy-start | bytes 3145732
  7.2 6.3 %copy-start.1 = (bf16[1,128,1024]{2,1,0:T(8,128)(2,1)S(1)}, bf16[1,128,1024]{2,1,0:T(8,128)(2,1)}, u32[]{:S(2)}) copy-start(bf16[1,128,1024]{2,1,0:T(8,128)(2,1)} %param.19) | copy-start | bytes 786436
  7.2 65.2 %all-gather.2.cloned.1.call-start = ((), (), s32[]{:S(2)}) async-start(), calls=%async_computation.3 | async-start | bytes 8921088 | tf_op jit(solution)/shard_map/all_gather | solution.py:100
  14.6 9.6 %copy-start.7 = (s32[1,8,64]{2,1,0:T(8,128)S(1)}, s32[1,8,64]{2,1,0:T(8,128)}, u32[]{:S(2)}) copy-start(s32[1,8,64]{2,1,0:T(8,128)} %param.13) | copy-start | bytes 6148
  15.7 26.0 %all-to-all-start = ((bf16[8,32,1024]{2,1,0:T(8,128)(2,1)}), bf16[8,32,1024]{2,1,0:T(8,128)(2,1)S(1)}, u32[]{:S(2)}, u32[]{:S(2)}) async-start(bf16[8,32,1024]{2,1,0:T(8,128)(2,1)} %select_select_fusion), calls=%async_computation | async-start | bytes 1048576 | tf_op jit(solution)/shard_map/all_to_all | solution.py:134
  24.2 223.9 %reduce-scatter.2.cloned.1.call-start = ((), (), s32[]{:S(2)}) async-start(), calls=%async_computation.4 | async-start | bytes 8921088 | tf_op jit(solution)/shard_map/reduce_scatter | solution.py:160
  110.6 3.2 copy-start.2
  110.6 3.2 copy-start.8
  113.8 1.6 copy-start.6
  132.6 3.6 %copy-start.4 = (bf16[256,1024]{1,0:T(8,128)(2,1)S(1)}, bf16[256,1024]{1,0:T(8,128)(2,1)}, u32[]{:S(2)}) copy-start(bf16[256,1024]{1,0:T(8,128)(2,1)} %reshape.305) | copy-start | bytes 1572868
  132.6 3.6 %copy-start.5 = (bf16[8,32,1024]{2,1,0:T(8,128)(2,1)S(1)}, bf16[8,32,1024]{2,1,0:T(8,128)(2,1)}, u32[]{:S(2)}) copy-start(bf16[8,32,1024]{2,1,0:T(8,128)(2,1)} %broadcast_select_fusion.1) | copy-start | bytes 1572868
  136.1 1.4 copy-start.3
  153.4 94.7 %all-to-all-start.1 = ((bf16[8,32,2048]{2,1,0:T(8,128)(2,1)}), bf16[8,32,2048]{2,1,0:T(8,128)(2,1)S(1)}, u32[]{:S(2)}, u32[]{:S(2)}) async-start(bf16[8,32,2048]{2,1,0:T(8,128)(2,1)} %broadcast_select_fusion), calls=%async_computation.1 | async-start | bytes 2097152 | tf_op jit(solution)/shard_map/all_to_all | solution.py:141
  160.4 162.8 %all-reduce.2.cloned.1.call-start = ((), (), s32[]{:S(2)}) async-start(), calls=%async_computation.5 | async-start | bytes 540672 | tf_op jit(solution)/shard_map/psum | solution.py:161
Sparse Core Ops, SparseCore 0:
  11.1 61.2 all-gather.1
  147.3 100.6 reduce-scatter.1
  250.4 72.8 all-reduce.1
where the time goes:
time: 336 us; the launch traced here: 335 us
  waiting for transfers between devices  203 us (60%)
  matrix products  44 us (13%)
  local copies, waits for them, and re-layouts  41.1 us (12%)
  other arithmetic  17.3 us (5%)
  starting transfers between devices  15.6 us (5%)
  between operations  14.1 us (4%)
    reduce_scatter x1, waiting for transfers between devices, on_device(): lax.psum_scatter(partial, 'replica', scatter_dimension=0, tiled=True)  87.6 us
    psum x1, waiting for transfers between devices, on_device(): summed = lax.psum(summed, 'batch').astype(jnp.float32)  72.4 us
    all_gather x1, waiting for transfers between devices, on_device(): lax.all_gather(jnp.concatenate([qkv_weight, out_weight, gain_block], axis...  29.1 us
    all_to_all x1, waiting for transfers between devices, on_device(): lax.all_to_all(backward_rows, 'batch', split_axis=0, concat_axis=0, tiled...  13.4 us
    all_to_all x1, starting transfers between devices, on_device(): lax.all_to_all(backward_rows, 'batch', split_axis=0, concat_axis=0, tiled...  8.47 us
    all_to_all x1, starting transfers between devices, on_device(): lax.all_to_all(jnp.take(jnp.concatenate([result, d_tokens], axis=-1), to_...  7.02 us
  transfers between devices with their start and end apart: 5, of which 4 were waited for; matrix products, arithmetic and copies ran while one was open for 6% of the time, Pallas kernels for 0%

commit v1 on v0

--- a/solution.py
+++ b/solution.py
@@ -158,7 +158,7 @@
         axis=1,
     )
     summed = lax.psum_scatter(partial, "replica", scatter_dimension=0, tiled=True)
-    summed = lax.psum(summed, "batch").astype(jnp.float32)
+    summed = lax.all_gather(summed, axis_name="batch").sum(axis=0).astype(jnp.float32)
     grad_q = summed[:, :qkv_cols]
     grad_o = summed[:, qkv_cols : qkv_cols + out_cols]
     grad_g = summed[:, qkv_cols + out_cols]

time: 336 us -> 308 us (0.917)
  waiting for transfers between devices: 203 us -> 151 us
  blocking collectives: 0 us -> 44.4 us
  local copies, waits for them, and re-layouts: 41.1 us -> 31 us
  starting transfers between devices: 15.6 us -> 8.58 us
    psum x1 -> x0, waiting for transfers between devices: 72.4 us -> none  [on_device(): summed = lax.psum(summed, 'batch').astype(jnp.float32)]
    all_to_all x0 -> x1, blocking collectives: none -> 44.4 us  [on_device(): lax.all_to_all(jnp.take(jnp.concatenate([result, d_tokens], axis=-1), to_...]
    reduce_scatter x1, waiting for transfers between devices: 87.6 us -> 101 us  [on_device(): lax.psum_scatter(partial, 'replica', scatter_dimension=0, tiled=True)]
    all_gather x0 -> x1, waiting for transfers between devices: none -> 7.46 us  [on_device(): lax.all_gather(summed, axis_name='batch').sum(axis=0).astype(jnp.float32)]
    all_to_all x1 -> x0, starting transfers between devices: 7.02 us -> none  [on_device(): lax.all_to_all(jnp.take(jnp.concatenate([result, d_tokens], axis=-1), to_...]
  transfers between devices with their start and end apart: 5 -> 4, of which waited for: 4 -> 4; matrix products, arithmetic and copies ran while one was open for 6% -> 6% of each run, Pallas kernels for 0% -> 0%
where the time goes in v1:
time: 308 us; the launch traced here: 307 us
  waiting for transfers between devices  151 us (49%)
  blocking collectives  44.4 us (14%)
  matrix products  42.3 us (14%)
  local copies, waits for them, and re-layouts  31 us (10%)
  other arithmetic  16.2 us (5%)
  between operations  14.1 us (5%)
  starting transfers between devices  8.58 us (3%)
    reduce_scatter x1, waiting for transfers between devices, on_device(): lax.psum_scatter(partial, 'replica', scatter_dimension=0, tiled=True)  101 us
    all_to_all x1, blocking collectives, on_device(): lax.all_to_all(jnp.take(jnp.concatenate([result, d_tokens], axis=-1), to_...  44.4 us
    all_gather x1, waiting for transfers between devices, on_device(): lax.all_gather(jnp.concatenate([qkv_weight, out_weight, gain_block], axis...  29.1 us
    all_to_all x1, waiting for transfers between devices, on_device(): lax.all_to_all(backward_rows, 'batch', split_axis=0, concat_axis=0, tiled...  13.4 us
    all_to_all x1, starting transfers between devices, on_device(): lax.all_to_all(backward_rows, 'batch', split_axis=0, concat_axis=0, tiled...  8.47 us
    all_gather x1, waiting for transfers between devices, on_device(): lax.all_gather(summed, axis_name='batch').sum(axis=0).astype(jnp.float32)  7.46 us
  transfers between devices with their start and end apart: 4, of which 4 were waited for; matrix products, arithmetic and copies ran while one was open for 6% of the time, Pallas kernels for 0%

profile of v1, /device:TPU:2, one launch (start us, length us, event | category | flops | bytes accessed | tf_op | source)
XLA Modules:
  0.0 307.1 jit_solution(5081303758662866374)
XLA Ops:
  7.2 0.8 broadcast_in_dim.165
  8.1 1.7 pad_maximum_fusion.2
  10.3 1.3 reduce.14
  11.7 1.3 reduce.13
  13.5 1.2 gather_fusion
  14.7 1.0 select_select_fusion
  15.7 8.5 %all-to-all-start = ((bf16[8,32,1024]{2,1,0:T(8,128)(2,1)}), bf16[8,32,1024]{2,1,0:T(8,128)(2,1)S(1)}, u32[]{:S(2)}, u32[]{:S(2)}) async-start(bf16[8,32,1024]{2,1,0:T(8,128)(2,1)} %select_select_fusion), calls=%async_computation | async-start | bytes 1048576 | tf_op jit(solution)/shard_map/all_to_all | solution.py:134
  24.3 2.8 gather_fusion.3
  28.2 13.4 %all-to-all-done = bf16[8,32,1024]{2,1,0:T(8,128)(2,1)S(1)} async-done(((bf16[8,32,1024]{2,1,0:T(8,128)(2,1)}), bf16[8,32,1024]{2,1,0:T(8,128)(2,1)S(1)}, u32[]{:S(2)}, u32[]{:S(2)}) %all-to-all-start) | async-done | bytes 524320 | tf_op jit(solution)/shard_map/all_to_all | solution.py:134
  42.2 0.9 broadcast_select_fusion.1
  43.3 29.1 %all-gather.4.cloned.1.call-done = bf16[1024,4224]{1,0:T(8,128)(2,1)} async-done(((bf16[32,4224]{1,0:T(8,128)(2,1)}), bf16[1024,4224]{1,0:T(8,128)(2,1)}) %all-gather.4.cloned.1.call-update) | async-done | bytes 8650768 | tf_op jit(solution)/shard_map/all_gather | solution.py:100
  72.4 2.3 fusion.43
  75.4 1.1 convert_reduce_fusion.1
  76.5 4.7 %fusion.6 = bf16[256,3072]{1,0:T(8,128)(2,1)S(1)} fusion(bf16[1024,4224]{1,0:T(8,128)(2,1)} %all-gather.4.cloned.1.call-done, f32[1024]{0:T(1024)S(1)} %convert_reduce_fusion.1, f32[256]{0:T(256)S(1)} %rsqrt.12, f32[256]{0:T(256)S(1)} %div.51, bf16[256,1024]{1,0:T(8,128)(2,1)S(1)} %gather_fusion.3, pred[256]{0:T(512)(128)(4,1)S(1)} %compare_and_fusion.4), kind=kOutput, calls=%fused_computation.14 | convolution fusion | flops 1612972032 | bytes 8395008 | tf_op jit(solution)/shard_map/dot_general | solution.py:27
  81.3 0.9 fusion.109
  82.2 2.5 reshape.302
  84.7 1.6 reshape.304
  86.4 1.6 reshape.303
  88.0 3.2 %fusion.66 = f32[8,16,32,32]{2,3,1,0:T(8,128)} fusion(bf16[8,32,16,64]{3,2,1,0:T(8,128)(2,1)S(1)} %reshape.307, bf16[8,32,16,64]{3,2,1,0:T(8,128)(2,1)} %reshape.302), kind=kOutput, calls=%fused_computation.65 | convolution fusion | flops 16777216 | bytes 1572864 | tf_op jit(solution)/shard_map/gqhd,gkhd->ghqk/dot_general | solution.py:51
  91.2 4.1 %fusion.111 = (f32[8,16,32]{2,1,0:T(8,128)S(1)}, f32[8,16,32,32]{2,3,1,0:T(8,128)}) fusion(pred[8,32]{1,0:T(8,128)(4,1)S(1)} %iota_compare_fusion.3, bf16[8,32,16,64]{3,2,1,0:T(8,128)(2,1)} %reshape.304, bf16[8,32,16,64]{3,2,1,0:T(8,128)(2,1)} %reshape.303), kind=kOutput, calls=%fused_computation.155 | convolution fusion | flops 17301536 | bytes 1589504 | tf_op jit(solution)/shard_map/sub | solution.py:34
  95.3 5.8 %fusion.34 = bf16[8,32,16,64]{3,1,2,0:T(8,128)(2,1)} fusion(f32[8,16,32,32]{2,3,1,0:T(8,128)} %fusion.66, bf16[8,32,16,64]{3,2,1,0:T(8,128)(2,1)} %reshape.304, f32[8,16,32,32]{2,3,1,0:T(8,128)} %get-tuple-element.37, f32[8,16,32]{2,1,0:T(8,128)S(1)} %get-tuple-element.36), kind=kOutput, calls=%fused_computation.35 | convolution fusion | flops 17960992 | bytes 2113536 | tf_op jit(solution)/shard_map/ghqk,gkhd->gqhd/dot_general | solution.py:55
  101.0 5.6 %fusion.31 = bf16[8,32,16,64]{3,1,2,0:T(8,128)(2,1)} fusion(f32[8,16,32,32]{2,3,1,0:T(8,128)} %fusion.66, bf16[8,32,16,64]{3,2,1,0:T(8,128)(2,1)} %reshape.303, f32[8,16,32,32]{2,3,1,0:T(8,128)} %get-tuple-element.37, f32[8,16,32]{2,1,0:T(8,128)S(1)} %get-tuple-element.36), kind=kOutput, calls=%fused_computation.34 | convolution fusion | flops 17960992 | bytes 2113536 | tf_op jit(solution)/shard_map/ghqk,gqhd->gkhd/dot_general | solution.py:58
  106.7 3.2 %fusion.30 = bf16[8,32,16,64]{3,1,2,0:T(8,128)(2,1)} fusion(bf16[8,32,16,64]{3,2,1,0:T(8,128)(2,1)S(1)} %reshape.307, f32[8,16,32,32]{2,3,1,0:T(8,128)} %get-tuple-element.37, f32[8,16,32]{2,1,0:T(8,128)S(1)} %get-tuple-element.36), kind=kOutput, calls=%fused_computation.33 | convolution fusion | flops 17301504 | bytes 1589248 | tf_op jit(solution)/shard_map/ghqk,gqhd->gkhd/dot_general | solution.py:48
  109.9 1.6 fusion.29
  111.9 0.7 reshape.308
  112.6 0.9 constant_dynamic-update-slice_fusion.2
  113.5 1.6 copy.50
  115.1 0.7 reshape.309
  115.9 1.6 copy.52
  117.5 0.7 reshape.310
  118.2 1.6 copy.43
  119.9 1.5 reshape.305
  121.4 0.9 constant_dynamic-update-slice_fusion.1
  122.3 0.9 constant_dynamic-update-slice_fusion
  123.2 3.8 %convolution_convert_fusion = bf16[1024,3072]{1,0:T(8,128)(2,1)S(1)} fusion(bf16[256,3072]{1,0:T(8,128)(2,1)} %constant_dynamic-update-slice_fusion, f32[1024]{0:T(1024)S(1)} %convert_reduce_fusion.1, f32[256]{0:T(256)S(1)} %rsqrt.12, f32[256]{0:T(256)S(1)} %div.51, bf16[256,1024]{1,0:T(8,128)(2,1)S(1)} %gather_fusion.3, pred[256]{0:T(512)(128)(4,1)S(1)} %compare_and_fusion.4), kind=kOutput, calls=%fused_computation.9 | convolution fusion | flops 1615331328 | bytes 8395008 | tf_op jit(solution)/shard_map/dot_general | solution.py:89
  127.0 0.8 convolution_convert_fusion.1
  128.4 4.9 %fusion.57 = (bf16[1024]{0:T(1024)(128)(2,1)S(1)}, f32[256]{0:T(256)S(1)}, f32[256]{0:T(256)S(1)}, f32[256,1024]{1,0:T(8,128)S(1)}) fusion(f32[256]{0:T(256)S(1)} %rsqrt.12, f32[256]{0:T(256)S(1)} %div.51, bf16[256,1024]{1,0:T(8,128)(2,1)S(1)} %gather_fusion.3, pred[256]{0:T(512)(128)(4,1)S(1)} %compare_and_fusion.4, f32[1024]{0:T(1024)S(1)} %convert_reduce_fusion.1, ...), kind=kOutput, calls=%fused_computation.53 | convolution fusion | flops 1613232640 | bytes 9447680 | tf_op jit(solution)/shard_map/dot_general | solution.py:65
  133.5 3.7 %pad_maximum_fusion = bf16[1024,4224]{1,0:T(8,128)(2,1)} fusion(bf16[1024,128]{1,0:T(8,128)(2,1)S(1)} %broadcast_in_dim.181, bf16[1024,1024]{1,0:T(8,128)(2,1)S(1)} %convolution_convert_fusion.1, bf16[1024,3072]{1,0:T(8,128)(2,1)S(1)} %convolution_convert_fusion), kind=kLoop, calls=%fused_computation.8 | loop fusion | flops 25952256 | bytes 17301504 | tf_op jit(solution)/shard_map/concatenate | solution.py:152
  137.5 100.6 %reduce-scatter.2.cloned.1.call-done = bf16[32,4224]{1,0:T(8,128)(2,1)} async-done(((bf16[1024,4224]{1,0:T(8,128)(2,1)}), bf16[32,4224]{1,0:T(8,128)(2,1)}) %reduce-scatter.2.cloned.1.call-update) | async-done | bytes 270352 | tf_op jit(solution)/shard_map/reduce_scatter | solution.py:160
  238.6 2.3 fusion.40
  241.8 44.4 %all_to_all.10 = bf16[8,32,2048]{2,1,0:T(8,128)(2,1)S(1)} all-to-all(bf16[8,32,2048]{2,1,0:T(8,128)(2,1)S(1)} %broadcast_select_fusion), channel_id=1, replica_groups=mesh['batch'=8,'replica'=32] {'batch'}, dimensions={0} | all-to-all | bytes 2097152 | tf_op jit(solution)/shard_map/all_to_all | solution.py:141
  286.3 0.9 gather_fusion.5
  287.2 0.9 gather_fusion.4
  288.0 0.9 select_bitcast_fusion
  288.9 7.5 %all-gather.6.cloned.1.call-done = bf16[256,4224]{1,0:T(8,128)(2,1)} async-done(((bf16[32,4224]{1,0:T(8,128)(2,1)}), bf16[256,4224]{1,0:T(8,128)(2,1)}) %all-gather.6.cloned.1.call-update) | async-done | bytes 2162704 | tf_op jit(solution)/shard_map/all_gather | solution.py:161
  296.4 2.0 reduce_sum.135
  298.4 0.8 slice.75
  299.2 0.7 slice.76
  (74 shorter events, 7.4 us)
Async XLA Ops:
  7.2 17.1 %copy-start = (bf16[1,8,64,1024]{3,2,1,0:T(8,128)(2,1)S(1)}, bf16[1,8,64,1024]{3,2,1,0:T(8,128)(2,1)}, u32[]{:S(2)}) copy-start(bf16[1,8,64,1024]{3,2,1,0:T(8,128)(2,1)} %param.12) | copy-start | bytes 3145732
  7.2 6.3 %copy-start.2 = (bf16[1,128,1024]{2,1,0:T(8,128)(2,1)S(1)}, bf16[1,128,1024]{2,1,0:T(8,128)(2,1)}, u32[]{:S(2)}) copy-start(bf16[1,128,1024]{2,1,0:T(8,128)(2,1)} %param.19) | copy-start | bytes 786436
  7.2 65.2 %all-gather.4.cloned.1.call-start = ((), (), s32[]{:S(2)}) async-start(), calls=%async_computation.3 | async-start | bytes 8921088 | tf_op jit(solution)/shard_map/all_gather | solution.py:100
  14.6 9.6 %copy-start.8 = (s32[1,8,64]{2,1,0:T(8,128)S(1)}, s32[1,8,64]{2,1,0:T(8,128)}, u32[]{:S(2)}) copy-start(s32[1,8,64]{2,1,0:T(8,128)} %param.13) | copy-start | bytes 6148
  15.7 26.0 %all-to-all-start = ((bf16[8,32,1024]{2,1,0:T(8,128)(2,1)}), bf16[8,32,1024]{2,1,0:T(8,128)(2,1)S(1)}, u32[]{:S(2)}, u32[]{:S(2)}) async-start(bf16[8,32,1024]{2,1,0:T(8,128)(2,1)} %select_select_fusion), calls=%async_computation | async-start | bytes 1048576 | tf_op jit(solution)/shard_map/all_to_all | solution.py:134
  24.2 213.9 %reduce-scatter.2.cloned.1.call-start = ((), (), s32[]{:S(2)}) async-start(), calls=%async_computation.4 | async-start | bytes 8921088 | tf_op jit(solution)/shard_map/reduce_scatter | solution.py:160
  106.7 3.2 %copy-start.3 = (bf16[8,32,16,64]{3,2,1,0:T(8,128)(2,1)S(1)}, bf16[8,32,16,64]{3,2,1,0:T(8,128)(2,1)}, u32[]{:S(2)}) copy-start(bf16[8,32,16,64]{3,2,1,0:T(8,128)(2,1)} %reshape.302) | copy-start | bytes 1572868
  106.7 3.2 %copy-start.9 = (f32[8,16,32,32]{2,3,1,0:T(8,128)S(1)}, f32[8,16,32,32]{2,3,1,0:T(8,128)}, u32[]{:S(2)}) copy-start(f32[8,16,32,32]{2,3,1,0:T(8,128)} %get-tuple-element.37) | copy-start | bytes 1572868
  109.9 1.6 copy-start.7
  123.2 3.8 %copy-start.5 = (bf16[256,1024]{1,0:T(8,128)(2,1)S(1)}, bf16[256,1024]{1,0:T(8,128)(2,1)}, u32[]{:S(2)}) copy-start(bf16[256,1024]{1,0:T(8,128)(2,1)} %reshape.305) | copy-start | bytes 1572868
  123.2 3.8 %copy-start.6 = (bf16[8,32,1024]{2,1,0:T(8,128)(2,1)S(1)}, bf16[8,32,1024]{2,1,0:T(8,128)(2,1)}, u32[]{:S(2)}) copy-start(bf16[8,32,1024]{2,1,0:T(8,128)(2,1)} %broadcast_select_fusion.1) | copy-start | bytes 1572868
  126.9 1.4 copy-start.4
  137.2 159.2 %all-gather.6.cloned.1.call-start = ((), (), s32[]{:S(2)}) async-start(), calls=%async_computation.5 | async-start | bytes 2433024 | tf_op jit(solution)/shard_map/all_gather | solution.py:161
  296.4 4.1 %copy-start.1 = (bf16[1,8,64,1024]{3,2,1,0:T(8,128)(2,1)S(1)}, bf16[1,8,64,1024]{3,2,1,0:T(8,128)(2,1)}, u32[]{:S(2)}) copy-start(bf16[1,8,64,1024]{3,2,1,0:T(8,128)(2,1)} %param.12) | copy-start | bytes 3145732
Sparse Core Ops, SparseCore 0:
  11.1 61.2 all-gather.3
  137.3 100.7 reduce-scatter.1
  239.9 56.4 all-gather.5
